TPU v7x, 32 devices: a whole 2x2x4 slice. The times are simulated.
32 devices in a mesh: groups: 2 (over x), tok: 16 (over z, y, core).
Axes of the slice: x: 2, y: 2, z: 4, core: 2. Of those that a mesh axis runs over, the one named last changes fastest.
Arguments:
- queries: bfloat16 [2, 8192, 1024], P(None, ('groups', 'tok')), parts along dimension 1, may hold values from -6 to 6
- keys: bfloat16 [2, 8192, 1024], P(None, ('groups', 'tok')), parts along dimension 1, may hold values from -6 to 6
- values: bfloat16 [2, 8192, 1024], P(None, ('groups', 'tok')), parts along dimension 1, may hold values from -6 to 6
- rates: float32 [2, 3, 2, 8192], P(None, None, None, ('groups', 'tok')), parts along dimension 3, may hold values from 0.0002 to 0.002
- fast_weights: float32 [2, 3, 512, 512], P(None, None, 'tok'), may hold values from -0.25 to 0.25
Outputs:
- attended: bfloat16 [2, 8192, 1024], P(None, ('groups', 'tok')), parts along dimension 1
- final_weights: float32 [4, 3, 512, 512], P('groups', None, 'tok'), parts along dimension 0
There are 2 independent parts, one for each index of `groups`. A program takes and returns all parts, laid end to end along the dimension named above; an argument that names none is the same for every part. Nothing has to cross between parts.
All inputs are finite; a program needn't handle non-finite values.
Results may differ from a plain program's by a relative error of at most 0.0098.
Values may be sent and summed in bfloat16 or wider, within the bound.
No kernel may reach another device: no remote copies, remote signals or barrier semaphores. Data moves between devices by JAX's collectives and lax.ppermute only.
A program may use at most 64 MiB of HBM per device.

v0:
```python
import jax
import jax.numpy as jnp
from jax import lax
from jax.sharding import PartitionSpec as P


def cross(left, right):
    return lax.dot_general(
        left, right, (((1,), (1,)), ((), ())), preferred_element_type=jnp.float32
    )


def inner(left, right):
    return lax.dot_general(
        left, right, (((0,), (0,)), ((), ())), preferred_element_type=jnp.float32
    )


def renorm(old, upd):
    old_norm = jnp.sqrt(jnp.mean(old * old, axis=-1))
    new_norm = jnp.sqrt(jnp.mean(upd * upd, axis=-1) + 1e-06)
    return upd * (old_norm / new_norm)[..., None]


def head_step(query, key_rows, value_rows, rate_rows, wbf):
    hidden_q = (jax.nn.silu(cross(query, wbf[0])) * cross(query, wbf[1])).astype(jnp.bfloat16)
    raw = cross(hidden_q, wbf[2])
    normed = (raw / jnp.sqrt(jnp.mean(raw * raw, axis=-1, keepdims=True) + 1e-06)).astype(
        jnp.bfloat16
    )
    h1 = cross(key_rows, wbf[0])
    h3 = cross(key_rows, wbf[1])
    sig = jax.nn.sigmoid(h1)
    act = h1 * sig
    back = jnp.dot(value_rows, wbf[2], preferred_element_type=jnp.float32)
    d1 = back * h3 * sig * (1.0 + h1 * (1.0 - sig))
    d3 = back * act
    e1 = (rate_rows[0][:, None] * d1).astype(jnp.bfloat16)
    e3 = (rate_rows[1][:, None] * d3).astype(jnp.bfloat16)
    b2 = (rate_rows[2][:, None] * (act * h3)).astype(jnp.bfloat16)
    grad = jnp.stack([inner(e1, key_rows), inner(e3, key_rows), inner(value_rows, b2)])
    return (normed, grad)


def block_step(span, gathered, queries, keys, values, rates):
    heads = gathered.shape[0]
    width = gathered.shape[3]
    pieces = []
    grads = []
    for head in range(heads):
        lo = head * width
        normed, grad = head_step(
            queries[span][:, lo : lo + width],
            keys[span][:, lo : lo + width],
            values[span][:, lo : lo + width],
            rates[span][:, head],
            gathered[head],
        )
        pieces.append(normed)
        grads.append(grad)
    return (jnp.concatenate(pieces, axis=1), jnp.stack(grads))


def fetch(own):
    return lax.all_gather(own.astype(jnp.bfloat16), "tok", axis=2, tiled=True)


def settle(partial_value, own):
    total = lax.psum_scatter(partial_value, "tok", scatter_dimension=2, tiled=True)
    return renorm(own, own + total)


def on_device(queries, keys, values, rates, fast_weights):
    nblocks = queries.shape[0]
    own = fast_weights
    blocks = []
    for span in range(nblocks):
        gathered = fetch(own)
        normed, partial_value = block_step(span, gathered, queries, keys, values, rates)
        blocks.append(normed)
        own = settle(partial_value, own)
    return (jnp.stack(blocks), own)


def solution(mesh):
    placed = (
        P(None, ("groups", "tok"), None),
        P(None, ("groups", "tok"), None),
        P(None, ("groups", "tok"), None),
        P(None, None, None, ("groups", "tok")),
        P(None, None, "tok", None),
    )
    return jax.shard_map(
        on_device,
        mesh=mesh,
        in_specs=placed,
        out_specs=(P(None, ("groups", "tok"), None), P("groups", None, "tok", None)),
        check_vma=False,
    )
```

profile of v0, /device:TPU:0, one launch (start us, length us, event | category | flops | bytes accessed | tf_op | source)
XLA Modules:
  0.0 308.0 jit_solution(13420339890189697955)
XLA Ops:
  7.2 1.9 multiply_reduce_fusion.7
  9.2 0.0 reduce-scatter.3.cloned.1.call-start
  9.2 0.7 slice_bitcast_fusion.46
  9.9 0.6 fusion.122
  10.5 2.2 slice_bitcast_fusion.12
  12.8 1.1 slice_bitcast_fusion.13
  13.8 45.2 %all-gather.3.cloned.1.call-done = bf16[2,3,512,512]{3,2,1,0:T(8,128)(2,1)} async-done(((bf16[2,3,32,512]{3,2,1,0:T(8,128)(2,1)}), bf16[2,3,512,512]{3,2,1,0:T(8,128)(2,1)}) %all-gather.3.cloned.1.call-update) | async-done | bytes 3145744 | tf_op jit(solution)/shard_map/all_gather | solution.py:65
  59.0 1.6 fusion.34
  60.6 1.4 fusion.37
  62.0 1.4 convolution_bitcast_fusion.10
  63.5 0.3 fusion.36
  63.8 0.5 convolution_bitcast_fusion.11
  64.3 0.2 copy-done.6
  64.5 0.4 convolution_bitcast_fusion.9
  65.0 0.3 fusion.38
  65.3 0.3 fusion.40
  65.6 0.4 convolution_bitcast_fusion.6
  66.1 0.3 fusion.41
  66.4 0.5 convolution_bitcast_fusion.8
  66.9 0.5 convolution_bitcast_fusion.7
  67.4 0.3 maximum_bitcast_fusion
  67.7 0.3 maximum_bitcast_fusion.1
  68.0 3.4 %pad_maximum_fusion = f32[2,3,512,512]{3,2,1,0:T(8,128)} fusion(f32[1,3,512,512]{3,2,1,0:T(8,128)S(1)} %maximum_bitcast_fusion.1, f32[1,3,512,512]{3,2,1,0:T(8,128)S(1)} %maximum_bitcast_fusion), kind=kLoop, calls=%fused_computation | loop fusion | flops 1572864 | bytes 12582912 | tf_op jit(solution)/shard_map/stack | solution.py:61
  71.4 0.0 all-gather.5.cloned.1.call-start
  71.5 83.5 %reduce-scatter.3.cloned.1.call-done = f32[2,3,32,512]{3,2,1,0:T(8,128)} async-done(((f32[2,3,512,512]{3,2,1,0:T(8,128)}), f32[2,3,32,512]{3,2,1,0:T(8,128)}) %reduce-scatter.3.cloned.1.call-update) | async-done | bytes 393232 | tf_op jit(solution)/shard_map/reduce_scatter | solution.py:69
  155.0 1.2 multiply_reduce_fusion.6
  156.2 0.8 multiply_convert_fusion.12
  157.0 0.2 reduce-scatter.5.cloned.1.call-start
  157.2 45.1 %all-gather.5.cloned.1.call-done = bf16[2,3,512,512]{3,2,1,0:T(8,128)(2,1)} async-done(((bf16[2,3,32,512]{3,2,1,0:T(8,128)(2,1)}), bf16[2,3,512,512]{3,2,1,0:T(8,128)(2,1)}) %all-gather.5.cloned.1.call-update) | async-done | bytes 3145744 | tf_op jit(solution)/shard_map/all_gather | solution.py:65
  202.4 1.6 convolution_bitcast_fusion.16
  204.0 1.4 convolution_bitcast_fusion.13
  205.4 1.4 convolution_bitcast_fusion.4
  206.9 0.3 convolution_bitcast_fusion.17
  207.2 0.5 convolution_bitcast_fusion.5
  207.8 0.1 copy-done.5
  207.9 0.4 convolution_bitcast_fusion.3
  208.3 0.3 convolution_bitcast_fusion.14
  208.7 0.3 convolution_bitcast_fusion.15
  209.0 0.4 convolution_bitcast_fusion
  209.5 0.3 convolution_bitcast_fusion.12
  209.8 0.5 convolution_bitcast_fusion.2
  210.3 0.5 convolution_bitcast_fusion.1
  210.8 0.3 maximum_bitcast_fusion.2
  211.1 0.3 maximum_bitcast_fusion.3
  211.4 3.4 %pad_maximum_fusion.1 = f32[2,3,512,512]{3,2,1,0:T(8,128)} fusion(f32[1,3,512,512]{3,2,1,0:T(8,128)S(1)} %maximum_bitcast_fusion.3, f32[1,3,512,512]{3,2,1,0:T(8,128)S(1)} %maximum_bitcast_fusion.2), kind=kLoop, calls=%fused_computation.1 | loop fusion | flops 1572864 | bytes 12582912 | tf_op jit(solution)/shard_map/stack | solution.py:61
  214.8 2.1 slice_bitcast_fusion.17
  216.9 0.8 copy-done.7
  217.6 1.2 fusion.39
  218.8 2.5 multiply_reduce_fusion.2
  221.3 2.1 fusion.35
  223.4 2.5 multiply_reduce_fusion.3
  226.0 1.6 divide_convert_fusion.2
  227.5 0.9 maximum_bitcast_fusion.4
  228.4 2.3 convolution_bitcast_fusion.19
  230.7 2.5 multiply_reduce_fusion
  233.2 2.1 convolution_bitcast_fusion.21
  235.3 2.5 multiply_reduce_fusion.1
  237.8 1.1 divide_convert_fusion
  239.0 1.1 divide_convert_fusion.1
  240.1 0.1 maximum_bitcast_fusion.5
  240.2 2.1 pad_maximum_fusion.2
  242.3 56.0 %reduce-scatter.5.cloned.1.call-done = f32[2,3,32,512]{3,2,1,0:T(8,128)} async-done(((f32[2,3,512,512]{3,2,1,0:T(8,128)}), f32[2,3,32,512]{3,2,1,0:T(8,128)}) %reduce-scatter.5.cloned.1.call-update) | async-done | bytes 393232 | tf_op jit(solution)/shard_map/reduce_scatter | solution.py:69
  298.3 1.2 multiply_reduce_fusion.5
  299.6 1.9 broadcast_multiply_fusion
  (32 shorter events, 0.2 us)
Async XLA Ops:
  7.2 5.6 %copy-start.8 = (bf16[2,256,1024]{2,1,0:T(8,128)(2,1)S(1)}, bf16[2,256,1024]{2,1,0:T(8,128)(2,1)}, u32[]{:S(2)}) copy-start(bf16[2,256,1024]{2,1,0:T(8,128)(2,1)} %param.7) | copy-start | bytes 3145732
  7.2 51.8 %all-gather.3.cloned.1.call-start = ((), (), s32[]{:S(2)}) async-start(), calls=%async_computation.2 | async-start | bytes 3342336 | tf_op jit(solution)/shard_map/all_gather | solution.py:65
  9.2 145.8 %reduce-scatter.3.cloned.1.call-start = ((), (), s32[]{:S(2)}) async-start(), calls=%async_computation.3 | async-start | bytes 6684672 | tf_op jit(solution)/shard_map/reduce_scatter | solution.py:69
  59.0 4.5 %copy-start = (bf16[2,3,512,512]{3,2,1,0:T(8,128)(2,1)S(1)}, bf16[2,3,512,512]{3,2,1,0:T(8,128)(2,1)}, u32[]{:S(2)}) copy-start(bf16[2,3,512,512]{3,2,1,0:T(8,128)(2,1)} %all-gather.3.cloned.1.call-done) | copy-start | bytes 9437188
  59.0 4.5 %copy-start.4 = (bf16[256,1024]{1,0:T(8,128)(2,1)S(1)}, bf16[256,1024]{1,0:T(8,128)(2,1)}, u32[]{:S(2)}) copy-start(bf16[256,1024]{1,0:T(8,128)(2,1)} %get-tuple-element.9) | copy-start | bytes 1572868
  63.5 1.0 copy-start.6
  71.4 131.0 %all-gather.5.cloned.1.call-start = ((), (), s32[]{:S(2)}) async-start(), calls=%async_computation.4 | async-start | bytes 3342336 | tf_op jit(solution)/shard_map/all_gather | solution.py:65
  157.0 141.3 %reduce-scatter.5.cloned.1.call-start = ((), (), s32[]{:S(2)}) async-start(), calls=%async_computation.5 | async-start | bytes 6684672 | tf_op jit(solution)/shard_map/reduce_scatter | solution.py:69
  202.4 4.5 %copy-start.1 = (bf16[2,3,512,512]{3,2,1,0:T(8,128)(2,1)S(1)}, bf16[2,3,512,512]{3,2,1,0:T(8,128)(2,1)}, u32[]{:S(2)}) copy-start(bf16[2,3,512,512]{3,2,1,0:T(8,128)(2,1)} %all-gather.5.cloned.1.call-done) | copy-start | bytes 9437188
  202.4 4.5 %copy-start.3 = (bf16[256,1024]{1,0:T(8,128)(2,1)S(1)}, bf16[256,1024]{1,0:T(8,128)(2,1)}, u32[]{:S(2)}) copy-start(bf16[256,1024]{1,0:T(8,128)(2,1)} %get-tuple-element.8) | copy-start | bytes 1572868
  204.0 3.2 %copy-start.11 = (f32[1,1,256]{2,1,0:T(1,128)S(1)}, f32[1,1,256]{2,1,0:T(1,128)}, u32[]{:S(2)}) copy-start(f32[1,1,256]{2,1,0:T(1,128)} %get-tuple-element.16) | copy-start | bytes 3076
  206.8 1.0 copy-start.5
  206.9 1.0 copy-start.10
  207.7 1.3 copy-start.9
  216.9 0.8 copy-start.7
  225.9 4.8 %copy-start.2 = (bf16[2,3,512,512]{3,2,1,0:T(8,128)(2,1)S(1)}, bf16[2,3,512,512]{3,2,1,0:T(8,128)(2,1)}, u32[]{:S(2)}) copy-start(bf16[2,3,512,512]{3,2,1,0:T(8,128)(2,1)} %all-gather.5.cloned.1.call-done) | copy-start | bytes 9437188
Sparse Core Ops, SparseCore 0:
  10.7 48.2 all-gather.2
  71.5 83.3 reduce-scatter.2
  157.7 44.6 all-gather.4
  214.9 83.3 reduce-scatter.4
where the time goes:
time: 309 us; the launch traced here: 308 us
  waiting for transfers between devices  230 us (74%)
  matrix products  33.9 us (11%)
  other arithmetic  22 us (7%)
  between operations  14.1 us (5%)
  local copies, waits for them, and re-layouts  7.79 us (3%)
    reduce_scatter x2, waiting for transfers between devices, settle(): lax.psum_scatter(partial_value, 'tok', scatter_dimension=2, tiled=True)  140 us
    all_gather x2, waiting for transfers between devices, fetch(): return lax.all_gather(own.astype(jnp.bfloat16), 'tok', axis=2, tiled=True)  90.3 us
    dot_general x16, matrix products, cross(): lax.dot_general(left, right, (((1,), (1,)), ((), ())), preferred_element_...  22.8 us
    another operation x6, other arithmetic, block_step(): return (jnp.concatenate(pieces, axis=1), jnp.stack(grads))  7.97 us
    dot_general x12, matrix products, inner(): lax.dot_general(left, right, (((0,), (0,)), ((), ())), preferred_element_...  7.62 us
  transfers between devices with their start and end apart: 4, of which 4 were waited for; matrix products, arithmetic and copies ran while one was open for 10% of the time, Pallas kernels for 0%

commit v1 on v0

--- a/solution.py
+++ b/solution.py
@@ -2,6 +2,7 @@
 import jax.numpy as jnp
 from jax import lax
 from jax.sharding import PartitionSpec as P
+from jax.lax import axis_index, axis_size, ppermute
 
 
 def cross(left, right):
@@ -62,7 +63,36 @@
 
 
 def fetch(own):
-    return lax.all_gather(own.astype(jnp.bfloat16), "tok", axis=2, tiled=True)
+
+    def _group_steps_all(u):
+        link_axis = "tok"
+        o_now = axis_size(link_axis)
+        row_out = axis_index(link_axis)
+        u_next, far_arr, mid_arr = (o_now, row_out, u.shape[2])
+        carry_out = jnp.zeros(
+            [tick * u_next if num == 2 else tick for num, tick in enumerate(u.shape)], u.dtype
+        )
+        met_up = lax.dynamic_update_slice_in_dim(carry_out, u, far_arr * mid_arr, axis=2)
+        base_arr = r_now = u
+        for s in range(1, u_next // 2 + 1):
+            base_arr = ppermute(
+                base_arr, link_axis, list(map(lambda num: (num, (num + 1) % u_next), range(u_next)))
+            )
+            met_up = lax.dynamic_update_slice_in_dim(
+                met_up, base_arr, (far_arr - s) % u_next * mid_arr, axis=2
+            )
+            if 2 * s < u_next:
+                r_now = ppermute(
+                    r_now,
+                    link_axis,
+                    list(map(lambda num: (num, (num - 1) % u_next), range(u_next))),
+                )
+                met_up = lax.dynamic_update_slice_in_dim(
+                    met_up, r_now, (far_arr + s) % u_next * mid_arr, axis=2
+                )
+        return met_up
+
+    return _group_steps_all(own.astype(jnp.bfloat16))
 
 
 def settle(partial_value, own):

time: 309 us -> 333 us (1.078)
  starting transfers between devices: 0.34 us -> 63.8 us
  waiting for transfers between devices: 230 us -> 194 us
  matrix products: 33.9 us -> 29.5 us
    all_gather x2 -> x0, waiting for transfers between devices: 90.3 us -> none  [fetch(): return lax.all_gather(own.astype(jnp.bfloat16), 'tok', axis=2, tiled=True)]
    ppermute x0 -> x30, starting transfers between devices: none -> 63.7 us  [the longest x14 63.1 us: _group_steps_all(): ppermute(r_now, link_axis, list(map(lambda num: (num, (num - 1) % u_next)...]
    ppermute x0 -> x30, waiting for transfers between devices: none -> 58.9 us  [the longest x16 58.9 us: _group_steps_all(): ppermute(base_arr, link_axis, list(map(lambda num: (num, (num + 1) % u_ne...]
    reduce_scatter x2, waiting for transfers between devices: 140 us -> 136 us  [settle(): lax.psum_scatter(partial_value, 'tok', scatter_dimension=2, tiled=True)]
  transfers between devices with their start and end apart: 4 -> 32, of which waited for: 4 -> 17; matrix products, arithmetic and copies ran while one was open for 10% -> 11% of each run, Pallas kernels for 0% -> 0%
where the time goes in v1:
time: 333 us; the launch traced here: 332 us
  waiting for transfers between devices  194 us (58%)
  starting transfers between devices  63.8 us (19%)
  matrix products  29.5 us (9%)
  other arithmetic  19.9 us (6%)
  between operations  14.7 us (4%)
  local copies, waits for them, and re-layouts  9.81 us (3%)
    reduce_scatter x2, waiting for transfers between devices, settle(): lax.psum_scatter(partial_value, 'tok', scatter_dimension=2, tiled=True)  136 us
    ppermute x14, starting transfers between devices, _group_steps_all(): ppermute(r_now, link_axis, list(map(lambda num: (num, (num - 1) % u_next)...  63.1 us
    ppermute x16, waiting for transfers between devices, _group_steps_all(): ppermute(base_arr, link_axis, list(map(lambda num: (num, (num + 1) % u_ne...  58.9 us
    dot_general x16, matrix products, cross(): lax.dot_general(left, right, (((1,), (1,)), ((), ())), preferred_element_...  23.3 us
    another operation x6, other arithmetic, block_step(): return (jnp.concatenate(pieces, axis=1), jnp.stack(grads))  7.92 us
  transfers between devices with their start and end apart: 32, of which 17 were waited for; matrix products, arithmetic and copies ran while one was open for 11% of the time, Pallas kernels for 0%

profile of v1, /device:TPU:0, one launch (start us, length us, event | category | flops | bytes accessed | tf_op | source)
XLA Modules:
  0.0 332.2 jit_solution(9403013032408039528)
XLA Ops:
  7.5 0.7 copy-done.5
  8.2 0.7 constant_dynamic-update-slice_fusion.31
  8.9 0.5 collective-permute-start
  9.4 5.0 %collective-permute-start.1 = (bf16[2,3,32,512]{3,2,1,0:T(8,128)(2,1)}, bf16[2,3,32,512]{3,2,1,0:T(8,128)(2,1)S(1)}, u32[]{:S(2)}, u32[]{:S(2)}) collective-permute-start(bf16[2,3,32,512]{3,2,1,0:T(8,128)(2,1)} %get-tuple-element.9), channel_id=1, source_target_pairs={{0,15},{1,0},{2,1},{3,2},{4,3},{5,4},{6,5},{7,6},{8,7},{9,8},{10,9... | collective-permute-start | bytes 589832 | tf_op jit(solution)/shard_map/ppermute | solution.py:85
  14.4 0.7 slice_bitcast_fusion.58
  15.1 2.2 slice_bitcast_fusion.12
  17.3 2.2 slice_bitcast_fusion.13
  19.5 0.6 fusion.88
  20.2 4.4 %collective-permute-start.3 = (bf16[2,3,32,512]{3,2,1,0:T(8,128)(2,1)S(1)}, bf16[2,3,32,512]{3,2,1,0:T(8,128)(2,1)S(1)}, u32[]{:S(2)}, u32[]{:S(2)}) collective-permute-start(bf16[2,3,32,512]{3,2,1,0:T(8,128)(2,1)S(1)} %collective-permute-done.1), channel_id=1, source_target_pairs={{0,15},{1,0},{2,1},{3,2},{4,3},{5,4},{6,5},{7,6},{8,7},{9,8},{10,9... | collective-permute-start | bytes 589832 | tf_op jit(solution)/shard_map/ppermute | solution.py:85
  24.7 3.3 collective-permute-done.2
  28.0 4.5 %collective-permute-start.5 = (bf16[2,3,32,512]{3,2,1,0:T(8,128)(2,1)S(1)}, bf16[2,3,32,512]{3,2,1,0:T(8,128)(2,1)S(1)}, u32[]{:S(2)}, u32[]{:S(2)}) collective-permute-start(bf16[2,3,32,512]{3,2,1,0:T(8,128)(2,1)S(1)} %collective-permute-done.3), channel_id=1, source_target_pairs={{0,15},{1,0},{2,1},{3,2},{4,3},{5,4},{6,5},{7,6},{8,7},{9,8},{10,9... | collective-permute-start | bytes 589832 | tf_op jit(solution)/shard_map/ppermute | solution.py:85
  32.6 3.3 collective-permute-done.4
  35.9 4.5 %collective-permute-start.7 = (bf16[2,3,32,512]{3,2,1,0:T(8,128)(2,1)S(1)}, bf16[2,3,32,512]{3,2,1,0:T(8,128)(2,1)S(1)}, u32[]{:S(2)}, u32[]{:S(2)}) collective-permute-start(bf16[2,3,32,512]{3,2,1,0:T(8,128)(2,1)S(1)} %collective-permute-done.5), channel_id=1, source_target_pairs={{0,15},{1,0},{2,1},{3,2},{4,3},{5,4},{6,5},{7,6},{8,7},{9,8},{10,9... | collective-permute-start | bytes 589832 | tf_op jit(solution)/shard_map/ppermute | solution.py:85
  40.5 3.3 collective-permute-done.6
  43.8 4.5 %collective-permute-start.9 = (bf16[2,3,32,512]{3,2,1,0:T(8,128)(2,1)S(1)}, bf16[2,3,32,512]{3,2,1,0:T(8,128)(2,1)S(1)}, u32[]{:S(2)}, u32[]{:S(2)}) collective-permute-start(bf16[2,3,32,512]{3,2,1,0:T(8,128)(2,1)S(1)} %collective-permute-done.7), channel_id=1, source_target_pairs={{0,15},{1,0},{2,1},{3,2},{4,3},{5,4},{6,5},{7,6},{8,7},{9,8},{10,9... | collective-permute-start | bytes 589832 | tf_op jit(solution)/shard_map/ppermute | solution.py:85
  48.4 3.3 collective-permute-done.8
  51.7 4.4 %collective-permute-start.11 = (bf16[2,3,32,512]{3,2,1,0:T(8,128)(2,1)S(1)}, bf16[2,3,32,512]{3,2,1,0:T(8,128)(2,1)S(1)}, u32[]{:S(2)}, u32[]{:S(2)}) collective-permute-start(bf16[2,3,32,512]{3,2,1,0:T(8,128)(2,1)S(1)} %collective-permute-done.9), channel_id=1, source_target_pairs={{0,15},{1,0},{2,1},{3,2},{4,3},{5,4},{6,5},{7,6},{8,7},{9,8},{10,9... | collective-permute-start | bytes 589832 | tf_op jit(solution)/shard_map/ppermute | solution.py:85
  56.2 3.4 %collective-permute-done.10 = bf16[2,3,32,512]{3,2,1,0:T(8,128)(2,1)S(1)} collective-permute-done((bf16[2,3,32,512]{3,2,1,0:T(8,128)(2,1)S(1)}, bf16[2,3,32,512]{3,2,1,0:T(8,128)(2,1)S(1)}, u32[]{:S(2)}, u32[]{:S(2)}) %collective-permute-start.10) | collective-permute-done | bytes 196640 | tf_op jit(solution)/shard_map/ppermute | solution.py:78
  59.6 4.4 %collective-permute-start.13 = (bf16[2,3,32,512]{3,2,1,0:T(8,128)(2,1)S(1)}, bf16[2,3,32,512]{3,2,1,0:T(8,128)(2,1)S(1)}, u32[]{:S(2)}, u32[]{:S(2)}) collective-permute-start(bf16[2,3,32,512]{3,2,1,0:T(8,128)(2,1)S(1)} %collective-permute-done.11), channel_id=1, source_target_pairs={{0,15},{1,0},{2,1},{3,2},{4,3},{5,4},{6,5},{7,6},{8,7},{9,8},{10,9... | collective-permute-start | bytes 589832 | tf_op jit(solution)/shard_map/ppermute | solution.py:85
  64.1 3.3 collective-permute-done.12
  67.4 7.7 %collective-permute-done.14 = bf16[2,3,32,512]{3,2,1,0:T(8,128)(2,1)S(1)} collective-permute-done((bf16[2,3,32,512]{3,2,1,0:T(8,128)(2,1)S(1)}, bf16[2,3,32,512]{3,2,1,0:T(8,128)(2,1)S(1)}, u32[]{:S(2)}, u32[]{:S(2)}) %collective-permute-start.14) | collective-permute-done | bytes 196640 | tf_op jit(solution)/shard_map/ppermute | solution.py:78
  77.6 0.4 convolution_bitcast_fusion.11
  78.0 0.4 convolution_bitcast_fusion.9
  78.5 0.4 convolution_bitcast_fusion.6
  78.9 0.4 convolution_bitcast_fusion.8
  80.3 3.3 %pad_maximum_fusion = f32[2,3,512,512]{3,2,1,0:T(8,128)} fusion(f32[1,3,512,512]{3,2,1,0:T(8,128)S(1)} %maximum_bitcast_fusion.1, f32[1,3,512,512]{3,2,1,0:T(8,128)S(1)} %maximum_bitcast_fusion), kind=kLoop, calls=%fused_computation | loop fusion | flops 1572864 | bytes 12582912 | tf_op jit(solution)/shard_map/stack | solution.py:62
  83.8 82.9 %reduce-scatter.3.cloned.1.call-done = f32[2,3,32,512]{3,2,1,0:T(8,128)} async-done(((f32[2,3,512,512]{3,2,1,0:T(8,128)}), f32[2,3,32,512]{3,2,1,0:T(8,128)}) %reduce-scatter.3.cloned.1.call-update) | async-done | bytes 393232 | tf_op jit(solution)/shard_map/reduce_scatter | solution.py:99
  166.7 1.1 multiply_reduce_fusion.6
  168.3 4.4 %collective-permute-start.16 = (bf16[2,3,32,512]{3,2,1,0:T(8,128)(2,1)S(1)}, bf16[2,3,32,512]{3,2,1,0:T(8,128)(2,1)S(1)}, u32[]{:S(2)}, u32[]{:S(2)}) collective-permute-start(bf16[2,3,32,512]{3,2,1,0:T(8,128)(2,1)S(1)} %get-tuple-element.5), channel_id=1, source_target_pairs={{0,15},{1,0},{2,1},{3,2},{4,3},{5,4},{6,5},{7,6},{8,7},{9,8},{10,9... | collective-permute-start | bytes 589832 | tf_op jit(solution)/shard_map/ppermute | solution.py:85
  172.7 3.5 %collective-permute-done.15 = bf16[2,3,32,512]{3,2,1,0:T(8,128)(2,1)S(1)} collective-permute-done((bf16[2,3,32,512]{3,2,1,0:T(8,128)(2,1)S(1)}, bf16[2,3,32,512]{3,2,1,0:T(8,128)(2,1)S(1)}, u32[]{:S(2)}, u32[]{:S(2)}) %collective-permute-start.15) | collective-permute-done | bytes 196640 | tf_op jit(solution)/shard_map/ppermute | solution.py:78
  176.2 4.4 %collective-permute-start.18 = (bf16[2,3,32,512]{3,2,1,0:T(8,128)(2,1)S(1)}, bf16[2,3,32,512]{3,2,1,0:T(8,128)(2,1)S(1)}, u32[]{:S(2)}, u32[]{:S(2)}) collective-permute-start(bf16[2,3,32,512]{3,2,1,0:T(8,128)(2,1)S(1)} %collective-permute-done.16), channel_id=1, source_target_pairs={{0,15},{1,0},{2,1},{3,2},{4,3},{5,4},{6,5},{7,6},{8,7},{9,8},{10,9... | collective-permute-start | bytes 589832 | tf_op jit(solution)/shard_map/ppermute | solution.py:85
  180.7 3.4 %collective-permute-done.17 = bf16[2,3,32,512]{3,2,1,0:T(8,128)(2,1)S(1)} collective-permute-done((bf16[2,3,32,512]{3,2,1,0:T(8,128)(2,1)S(1)}, bf16[2,3,32,512]{3,2,1,0:T(8,128)(2,1)S(1)}, u32[]{:S(2)}, u32[]{:S(2)}) %collective-permute-start.17) | collective-permute-done | bytes 196640 | tf_op jit(solution)/shard_map/ppermute | solution.py:78
  184.1 4.4 %collective-permute-start.20 = (bf16[2,3,32,512]{3,2,1,0:T(8,128)(2,1)S(1)}, bf16[2,3,32,512]{3,2,1,0:T(8,128)(2,1)S(1)}, u32[]{:S(2)}, u32[]{:S(2)}) collective-permute-start(bf16[2,3,32,512]{3,2,1,0:T(8,128)(2,1)S(1)} %collective-permute-done.18), channel_id=1, source_target_pairs={{0,15},{1,0},{2,1},{3,2},{4,3},{5,4},{6,5},{7,6},{8,7},{9,8},{10,9... | collective-permute-start | bytes 589832 | tf_op jit(solution)/shard_map/ppermute | solution.py:85
  188.6 3.3 collective-permute-done.19
  191.9 4.5 %collective-permute-start.22 = (bf16[2,3,32,512]{3,2,1,0:T(8,128)(2,1)S(1)}, bf16[2,3,32,512]{3,2,1,0:T(8,128)(2,1)S(1)}, u32[]{:S(2)}, u32[]{:S(2)}) collective-permute-start(bf16[2,3,32,512]{3,2,1,0:T(8,128)(2,1)S(1)} %collective-permute-done.20), channel_id=1, source_target_pairs={{0,15},{1,0},{2,1},{3,2},{4,3},{5,4},{6,5},{7,6},{8,7},{9,8},{10,9... | collective-permute-start | bytes 589832 | tf_op jit(solution)/shard_map/ppermute | solution.py:85
  196.4 3.3 collective-permute-done.21
  199.7 4.4 %collective-permute-start.24 = (bf16[2,3,32,512]{3,2,1,0:T(8,128)(2,1)S(1)}, bf16[2,3,32,512]{3,2,1,0:T(8,128)(2,1)S(1)}, u32[]{:S(2)}, u32[]{:S(2)}) collective-permute-start(bf16[2,3,32,512]{3,2,1,0:T(8,128)(2,1)S(1)} %collective-permute-done.22), channel_id=1, source_target_pairs={{0,15},{1,0},{2,1},{3,2},{4,3},{5,4},{6,5},{7,6},{8,7},{9,8},{10,9... | collective-permute-start | bytes 589832 | tf_op jit(solution)/shard_map/ppermute | solution.py:85
  204.2 3.4 %collective-permute-done.23 = bf16[2,3,32,512]{3,2,1,0:T(8,128)(2,1)S(1)} collective-permute-done((bf16[2,3,32,512]{3,2,1,0:T(8,128)(2,1)S(1)}, bf16[2,3,32,512]{3,2,1,0:T(8,128)(2,1)S(1)}, u32[]{:S(2)}, u32[]{:S(2)}) %collective-permute-start.23) | collective-permute-done | bytes 196640 | tf_op jit(solution)/shard_map/ppermute | solution.py:78
  207.6 4.4 %collective-permute-start.26 = (bf16[2,3,32,512]{3,2,1,0:T(8,128)(2,1)S(1)}, bf16[2,3,32,512]{3,2,1,0:T(8,128)(2,1)S(1)}, u32[]{:S(2)}, u32[]{:S(2)}) collective-permute-start(bf16[2,3,32,512]{3,2,1,0:T(8,128)(2,1)S(1)} %collective-permute-done.24), channel_id=1, source_target_pairs={{0,15},{1,0},{2,1},{3,2},{4,3},{5,4},{6,5},{7,6},{8,7},{9,8},{10,9... | collective-permute-start | bytes 589832 | tf_op jit(solution)/shard_map/ppermute | solution.py:85
  212.1 3.4 %collective-permute-done.25 = bf16[2,3,32,512]{3,2,1,0:T(8,128)(2,1)S(1)} collective-permute-done((bf16[2,3,32,512]{3,2,1,0:T(8,128)(2,1)S(1)}, bf16[2,3,32,512]{3,2,1,0:T(8,128)(2,1)S(1)}, u32[]{:S(2)}, u32[]{:S(2)}) %collective-permute-start.25) | collective-permute-done | bytes 196640 | tf_op jit(solution)/shard_map/ppermute | solution.py:78
  215.5 4.4 %collective-permute-start.28 = (bf16[2,3,32,512]{3,2,1,0:T(8,128)(2,1)S(1)}, bf16[2,3,32,512]{3,2,1,0:T(8,128)(2,1)S(1)}, u32[]{:S(2)}, u32[]{:S(2)}) collective-permute-start(bf16[2,3,32,512]{3,2,1,0:T(8,128)(2,1)S(1)} %collective-permute-done.26), channel_id=1, source_target_pairs={{0,15},{1,0},{2,1},{3,2},{4,3},{5,4},{6,5},{7,6},{8,7},{9,8},{10,9... | collective-permute-start | bytes 589832 | tf_op jit(solution)/shard_map/ppermute | solution.py:85
  220.0 3.3 collective-permute-done.27
  223.4 7.7 %collective-permute-done.29 = bf16[2,3,32,512]{3,2,1,0:T(8,128)(2,1)S(1)} collective-permute-done((bf16[2,3,32,512]{3,2,1,0:T(8,128)(2,1)S(1)}, bf16[2,3,32,512]{3,2,1,0:T(8,128)(2,1)S(1)}, u32[]{:S(2)}, u32[]{:S(2)}) %collective-permute-start.29) | collective-permute-done | bytes 196640 | tf_op jit(solution)/shard_map/ppermute | solution.py:78
  233.6 0.4 convolution_bitcast_fusion.5
  234.1 0.4 convolution_bitcast_fusion.3
  235.0 0.4 convolution_bitcast_fusion.2
  236.4 3.3 %pad_maximum_fusion.1 = f32[2,3,512,512]{3,2,1,0:T(8,128)} fusion(f32[1,3,512,512]{3,2,1,0:T(8,128)S(1)} %maximum_bitcast_fusion.3, f32[1,3,512,512]{3,2,1,0:T(8,128)S(1)} %maximum_bitcast_fusion.2), kind=kLoop, calls=%fused_computation.1 | loop fusion | flops 1572864 | bytes 12582912 | tf_op jit(solution)/shard_map/stack | solution.py:62
  239.8 2.2 slice_bitcast_fusion.17
  242.0 2.3 convolution_bitcast_fusion.29
  244.3 3.2 multiply_reduce_fusion.2
  247.5 2.3 convolution_bitcast_fusion.31
  249.8 3.2 multiply_reduce_fusion.3
  253.0 1.4 divide_convert_fusion.2
  254.4 0.9 maximum_bitcast_fusion.4
  255.3 2.1 convolution_bitcast_fusion.19
  257.4 2.7 multiply_reduce_fusion
  260.1 2.1 convolution_bitcast_fusion.21
  262.2 2.8 multiply_reduce_fusion.1
  265.0 1.1 divide_convert_fusion
  266.1 1.1 divide_convert_fusion.1
  267.4 2.2 pad_maximum_fusion.2
  269.6 52.6 %reduce-scatter.5.cloned.1.call-done = f32[2,3,32,512]{3,2,1,0:T(8,128)} async-done(((f32[2,3,512,512]{3,2,1,0:T(8,128)}), f32[2,3,32,512]{3,2,1,0:T(8,128)}) %reduce-scatter.5.cloned.1.call-update) | async-done | bytes 393232 | tf_op jit(solution)/shard_map/reduce_scatter | solution.py:99
  322.2 1.2 multiply_reduce_fusion.5
  323.5 1.9 broadcast_multiply_fusion
  (120 shorter events, 8.7 us)
Async XLA Ops:
  7.2 1.0 copy-start.5
  7.2 159.5 %reduce-scatter.3.cloned.1.call-start = ((), (), s32[]{:S(2)}) async-start(), calls=%async_computation.2 | async-start | bytes 6684672 | tf_op jit(solution)/shard_map/reduce_scatter | solution.py:99
  8.9 11.3 %collective-permute-start = (bf16[2,3,32,512]{3,2,1,0:T(8,128)(2,1)}, bf16[2,3,32,512]{3,2,1,0:T(8,128)(2,1)S(1)}, u32[]{:S(2)}, u32[]{:S(2)}) collective-permute-start(bf16[2,3,32,512]{3,2,1,0:T(8,128)(2,1)} %get-tuple-element.9), channel_id=1, source_target_pairs={{0,1},{1,2},{2,3},{3,4},{4,5},{5,6},{6,7},{7,8},{8,9},{9,10},{10,1... | collective-permute-start | bytes 589832 | tf_op jit(solution)/shard_map/ppermute | solution.py:78
  9.4 10.8 %collective-permute-start.1 = (bf16[2,3,32,512]{3,2,1,0:T(8,128)(2,1)}, bf16[2,3,32,512]{3,2,1,0:T(8,128)(2,1)S(1)}, u32[]{:S(2)}, u32[]{:S(2)}) collective-permute-start(bf16[2,3,32,512]{3,2,1,0:T(8,128)(2,1)} %get-tuple-element.9), channel_id=1, source_target_pairs={{0,15},{1,0},{2,1},{3,2},{4,3},{5,4},{6,5},{7,6},{8,7},{9,8},{10,9... | collective-permute-start | bytes 589832 | tf_op jit(solution)/shard_map/ppermute | solution.py:85
  19.5 55.7 %copy-start.2 = (bf16[256,1024]{1,0:T(8,128)(2,1)S(1)}, bf16[256,1024]{1,0:T(8,128)(2,1)}, u32[]{:S(2)}) copy-start(bf16[256,1024]{1,0:T(8,128)(2,1)} %get-tuple-element.13) | copy-start | bytes 1572868
  20.1 7.9 %collective-permute-start.2 = (bf16[2,3,32,512]{3,2,1,0:T(8,128)(2,1)S(1)}, bf16[2,3,32,512]{3,2,1,0:T(8,128)(2,1)S(1)}, u32[]{:S(2)}, u32[]{:S(2)}) collective-permute-start(bf16[2,3,32,512]{3,2,1,0:T(8,128)(2,1)S(1)} %collective-permute-done), channel_id=1, source_target_pairs={{0,1},{1,2},{2,3},{3,4},{4,5},{5,6},{6,7},{7,8},{8,9},{9,10},{10,1... | collective-permute-start | bytes 589832 | tf_op jit(solution)/shard_map/ppermute | solution.py:78
  20.2 7.8 %collective-permute-start.3 = (bf16[2,3,32,512]{3,2,1,0:T(8,128)(2,1)S(1)}, bf16[2,3,32,512]{3,2,1,0:T(8,128)(2,1)S(1)}, u32[]{:S(2)}, u32[]{:S(2)}) collective-permute-start(bf16[2,3,32,512]{3,2,1,0:T(8,128)(2,1)S(1)} %collective-permute-done.1), channel_id=1, source_target_pairs={{0,15},{1,0},{2,1},{3,2},{4,3},{5,4},{6,5},{7,6},{8,7},{9,8},{10,9... | collective-permute-start | bytes 589832 | tf_op jit(solution)/shard_map/ppermute | solution.py:85
  28.0 7.9 %collective-permute-start.4 = (bf16[2,3,32,512]{3,2,1,0:T(8,128)(2,1)S(1)}, bf16[2,3,32,512]{3,2,1,0:T(8,128)(2,1)S(1)}, u32[]{:S(2)}, u32[]{:S(2)}) collective-permute-start(bf16[2,3,32,512]{3,2,1,0:T(8,128)(2,1)S(1)} %collective-permute-done.2), channel_id=1, source_target_pairs={{0,1},{1,2},{2,3},{3,4},{4,5},{5,6},{6,7},{7,8},{8,9},{9,10},{10,1... | collective-permute-start | bytes 589832 | tf_op jit(solution)/shard_map/ppermute | solution.py:78
  28.0 7.9 %collective-permute-start.5 = (bf16[2,3,32,512]{3,2,1,0:T(8,128)(2,1)S(1)}, bf16[2,3,32,512]{3,2,1,0:T(8,128)(2,1)S(1)}, u32[]{:S(2)}, u32[]{:S(2)}) collective-permute-start(bf16[2,3,32,512]{3,2,1,0:T(8,128)(2,1)S(1)} %collective-permute-done.3), channel_id=1, source_target_pairs={{0,15},{1,0},{2,1},{3,2},{4,3},{5,4},{6,5},{7,6},{8,7},{9,8},{10,9... | collective-permute-start | bytes 589832 | tf_op jit(solution)/shard_map/ppermute | solution.py:85
  35.9 7.9 %collective-permute-start.6 = (bf16[2,3,32,512]{3,2,1,0:T(8,128)(2,1)S(1)}, bf16[2,3,32,512]{3,2,1,0:T(8,128)(2,1)S(1)}, u32[]{:S(2)}, u32[]{:S(2)}) collective-permute-start(bf16[2,3,32,512]{3,2,1,0:T(8,128)(2,1)S(1)} %collective-permute-done.4), channel_id=1, source_target_pairs={{0,1},{1,2},{2,3},{3,4},{4,5},{5,6},{6,7},{7,8},{8,9},{9,10},{10,1... | collective-permute-start | bytes 589832 | tf_op jit(solution)/shard_map/ppermute | solution.py:78
  35.9 7.9 %collective-permute-start.7 = (bf16[2,3,32,512]{3,2,1,0:T(8,128)(2,1)S(1)}, bf16[2,3,32,512]{3,2,1,0:T(8,128)(2,1)S(1)}, u32[]{:S(2)}, u32[]{:S(2)}) collective-permute-start(bf16[2,3,32,512]{3,2,1,0:T(8,128)(2,1)S(1)} %collective-permute-done.5), channel_id=1, source_target_pairs={{0,15},{1,0},{2,1},{3,2},{4,3},{5,4},{6,5},{7,6},{8,7},{9,8},{10,9... | collective-permute-start | bytes 589832 | tf_op jit(solution)/shard_map/ppermute | solution.py:85
  43.8 7.9 %collective-permute-start.8 = (bf16[2,3,32,512]{3,2,1,0:T(8,128)(2,1)S(1)}, bf16[2,3,32,512]{3,2,1,0:T(8,128)(2,1)S(1)}, u32[]{:S(2)}, u32[]{:S(2)}) collective-permute-start(bf16[2,3,32,512]{3,2,1,0:T(8,128)(2,1)S(1)} %collective-permute-done.6), channel_id=1, source_target_pairs={{0,1},{1,2},{2,3},{3,4},{4,5},{5,6},{6,7},{7,8},{8,9},{9,10},{10,1... | collective-permute-start | bytes 589832 | tf_op jit(solution)/shard_map/ppermute | solution.py:78
  43.8 7.9 %collective-permute-start.9 = (bf16[2,3,32,512]{3,2,1,0:T(8,128)(2,1)S(1)}, bf16[2,3,32,512]{3,2,1,0:T(8,128)(2,1)S(1)}, u32[]{:S(2)}, u32[]{:S(2)}) collective-permute-start(bf16[2,3,32,512]{3,2,1,0:T(8,128)(2,1)S(1)} %collective-permute-done.7), channel_id=1, source_target_pairs={{0,15},{1,0},{2,1},{3,2},{4,3},{5,4},{6,5},{7,6},{8,7},{9,8},{10,9... | collective-permute-start | bytes 589832 | tf_op jit(solution)/shard_map/ppermute | solution.py:85
  51.7 7.9 %collective-permute-start.10 = (bf16[2,3,32,512]{3,2,1,0:T(8,128)(2,1)S(1)}, bf16[2,3,32,512]{3,2,1,0:T(8,128)(2,1)S(1)}, u32[]{:S(2)}, u32[]{:S(2)}) collective-permute-start(bf16[2,3,32,512]{3,2,1,0:T(8,128)(2,1)S(1)} %collective-permute-done.8), channel_id=1, source_target_pairs={{0,1},{1,2},{2,3},{3,4},{4,5},{5,6},{6,7},{7,8},{8,9},{9,10},{10,1... | collective-permute-start | bytes 589832 | tf_op jit(solution)/shard_map/ppermute | solution.py:78
  51.7 7.9 %collective-permute-start.11 = (bf16[2,3,32,512]{3,2,1,0:T(8,128)(2,1)S(1)}, bf16[2,3,32,512]{3,2,1,0:T(8,128)(2,1)S(1)}, u32[]{:S(2)}, u32[]{:S(2)}) collective-permute-start(bf16[2,3,32,512]{3,2,1,0:T(8,128)(2,1)S(1)} %collective-permute-done.9), channel_id=1, source_target_pairs={{0,15},{1,0},{2,1},{3,2},{4,3},{5,4},{6,5},{7,6},{8,7},{9,8},{10,9... | collective-permute-start | bytes 589832 | tf_op jit(solution)/shard_map/ppermute | solution.py:85
  59.6 7.8 %collective-permute-start.12 = (bf16[2,3,32,512]{3,2,1,0:T(8,128)(2,1)S(1)}, bf16[2,3,32,512]{3,2,1,0:T(8,128)(2,1)S(1)}, u32[]{:S(2)}, u32[]{:S(2)}) collective-permute-start(bf16[2,3,32,512]{3,2,1,0:T(8,128)(2,1)S(1)} %collective-permute-done.10), channel_id=1, source_target_pairs={{0,1},{1,2},{2,3},{3,4},{4,5},{5,6},{6,7},{7,8},{8,9},{9,10},{10,1... | collective-permute-start | bytes 589832 | tf_op jit(solution)/shard_map/ppermute | solution.py:78
  59.6 7.8 %collective-permute-start.13 = (bf16[2,3,32,512]{3,2,1,0:T(8,128)(2,1)S(1)}, bf16[2,3,32,512]{3,2,1,0:T(8,128)(2,1)S(1)}, u32[]{:S(2)}, u32[]{:S(2)}) collective-permute-start(bf16[2,3,32,512]{3,2,1,0:T(8,128)(2,1)S(1)} %collective-permute-done.11), channel_id=1, source_target_pairs={{0,15},{1,0},{2,1},{3,2},{4,3},{5,4},{6,5},{7,6},{8,7},{9,8},{10,9... | collective-permute-start | bytes 589832 | tf_op jit(solution)/shard_map/ppermute | solution.py:85
  64.1 12.5 %copy-start.4 = (bf16[256,1024]{1,0:T(8,128)(2,1)S(1)}, bf16[256,1024]{1,0:T(8,128)(2,1)}, u32[]{:S(2)}) copy-start(bf16[256,1024]{1,0:T(8,128)(2,1)} %get-tuple-element.11) | copy-start | bytes 1572868
  67.4 7.8 %collective-permute-start.14 = (bf16[2,3,32,512]{3,2,1,0:T(8,128)(2,1)S(1)}, bf16[2,3,32,512]{3,2,1,0:T(8,128)(2,1)S(1)}, u32[]{:S(2)}, u32[]{:S(2)}) collective-permute-start(bf16[2,3,32,512]{3,2,1,0:T(8,128)(2,1)S(1)} %collective-permute-done.12), channel_id=1, source_target_pairs={{0,1},{1,2},{2,3},{3,4},{4,5},{5,6},{6,7},{7,8},{8,9},{9,10},{10,1... | collective-permute-start | bytes 589832 | tf_op jit(solution)/shard_map/ppermute | solution.py:78
  75.2 1.7 copy-start
  83.7 83.0 %copy-start.6 = (f32[2,3,32,512]{3,2,1,0:T(8,128)S(1)}, f32[2,3,32,512]{3,2,1,0:T(8,128)}, u32[]{:S(2)}) copy-start(f32[2,3,32,512]{3,2,1,0:T(8,128)} %param.9) | copy-start | bytes 1179652
  83.7 238.5 %reduce-scatter.5.cloned.1.call-start = ((), (), s32[]{:S(2)}) async-start(), calls=%async_computation.3 | async-start | bytes 6684672 | tf_op jit(solution)/shard_map/reduce_scatter | solution.py:99
  168.2 62.9 %copy-start.1 = (bf16[256,1024]{1,0:T(8,128)(2,1)S(1)}, bf16[256,1024]{1,0:T(8,128)(2,1)}, u32[]{:S(2)}) copy-start(bf16[256,1024]{1,0:T(8,128)(2,1)} %get-tuple-element.12) | copy-start | bytes 1572868
  168.2 7.9 %collective-permute-start.15 = (bf16[2,3,32,512]{3,2,1,0:T(8,128)(2,1)S(1)}, bf16[2,3,32,512]{3,2,1,0:T(8,128)(2,1)S(1)}, u32[]{:S(2)}, u32[]{:S(2)}) collective-permute-start(bf16[2,3,32,512]{3,2,1,0:T(8,128)(2,1)S(1)} %get-tuple-element.5), channel_id=1, source_target_pairs={{0,1},{1,2},{2,3},{3,4},{4,5},{5,6},{6,7},{7,8},{8,9},{9,10},{10,1... | collective-permute-start | bytes 589832 | tf_op jit(solution)/shard_map/ppermute | solution.py:78
  168.3 7.9 %collective-permute-start.16 = (bf16[2,3,32,512]{3,2,1,0:T(8,128)(2,1)S(1)}, bf16[2,3,32,512]{3,2,1,0:T(8,128)(2,1)S(1)}, u32[]{:S(2)}, u32[]{:S(2)}) collective-permute-start(bf16[2,3,32,512]{3,2,1,0:T(8,128)(2,1)S(1)} %get-tuple-element.5), channel_id=1, source_target_pairs={{0,15},{1,0},{2,1},{3,2},{4,3},{5,4},{6,5},{7,6},{8,7},{9,8},{10,9... | collective-permute-start | bytes 589832 | tf_op jit(solution)/shard_map/ppermute | solution.py:85
  176.2 7.9 %collective-permute-start.17 = (bf16[2,3,32,512]{3,2,1,0:T(8,128)(2,1)S(1)}, bf16[2,3,32,512]{3,2,1,0:T(8,128)(2,1)S(1)}, u32[]{:S(2)}, u32[]{:S(2)}) collective-permute-start(bf16[2,3,32,512]{3,2,1,0:T(8,128)(2,1)S(1)} %collective-permute-done.15), channel_id=1, source_target_pairs={{0,1},{1,2},{2,3},{3,4},{4,5},{5,6},{6,7},{7,8},{8,9},{9,10},{10,1... | collective-permute-start | bytes 589832 | tf_op jit(solution)/shard_map/ppermute | solution.py:78
  176.2 7.9 %collective-permute-start.18 = (bf16[2,3,32,512]{3,2,1,0:T(8,128)(2,1)S(1)}, bf16[2,3,32,512]{3,2,1,0:T(8,128)(2,1)S(1)}, u32[]{:S(2)}, u32[]{:S(2)}) collective-permute-start(bf16[2,3,32,512]{3,2,1,0:T(8,128)(2,1)S(1)} %collective-permute-done.16), channel_id=1, source_target_pairs={{0,15},{1,0},{2,1},{3,2},{4,3},{5,4},{6,5},{7,6},{8,7},{9,8},{10,9... | collective-permute-start | bytes 589832 | tf_op jit(solution)/shard_map/ppermute | solution.py:85
  184.1 7.8 %collective-permute-start.19 = (bf16[2,3,32,512]{3,2,1,0:T(8,128)(2,1)S(1)}, bf16[2,3,32,512]{3,2,1,0:T(8,128)(2,1)S(1)}, u32[]{:S(2)}, u32[]{:S(2)}) collective-permute-start(bf16[2,3,32,512]{3,2,1,0:T(8,128)(2,1)S(1)} %collective-permute-done.17), channel_id=1, source_target_pairs={{0,1},{1,2},{2,3},{3,4},{4,5},{5,6},{6,7},{7,8},{8,9},{9,10},{10,1... | collective-permute-start | bytes 589832 | tf_op jit(solution)/shard_map/ppermute | solution.py:78
  184.1 7.8 %collective-permute-start.20 = (bf16[2,3,32,512]{3,2,1,0:T(8,128)(2,1)S(1)}, bf16[2,3,32,512]{3,2,1,0:T(8,128)(2,1)S(1)}, u32[]{:S(2)}, u32[]{:S(2)}) collective-permute-start(bf16[2,3,32,512]{3,2,1,0:T(8,128)(2,1)S(1)} %collective-permute-done.18), channel_id=1, source_target_pairs={{0,15},{1,0},{2,1},{3,2},{4,3},{5,4},{6,5},{7,6},{8,7},{9,8},{10,9... | collective-permute-start | bytes 589832 | tf_op jit(solution)/shard_map/ppermute | solution.py:85
  191.8 7.9 %collective-permute-start.21 = (bf16[2,3,32,512]{3,2,1,0:T(8,128)(2,1)S(1)}, bf16[2,3,32,512]{3,2,1,0:T(8,128)(2,1)S(1)}, u32[]{:S(2)}, u32[]{:S(2)}) collective-permute-start(bf16[2,3,32,512]{3,2,1,0:T(8,128)(2,1)S(1)} %collective-permute-done.19), channel_id=1, source_target_pairs={{0,1},{1,2},{2,3},{3,4},{4,5},{5,6},{6,7},{7,8},{8,9},{9,10},{10,1... | collective-permute-start | bytes 589832 | tf_op jit(solution)/shard_map/ppermute | solution.py:78
  191.9 7.9 %collective-permute-start.22 = (bf16[2,3,32,512]{3,2,1,0:T(8,128)(2,1)S(1)}, bf16[2,3,32,512]{3,2,1,0:T(8,128)(2,1)S(1)}, u32[]{:S(2)}, u32[]{:S(2)}) collective-permute-start(bf16[2,3,32,512]{3,2,1,0:T(8,128)(2,1)S(1)} %collective-permute-done.20), channel_id=1, source_target_pairs={{0,15},{1,0},{2,1},{3,2},{4,3},{5,4},{6,5},{7,6},{8,7},{9,8},{10,9... | collective-permute-start | bytes 589832 | tf_op jit(solution)/shard_map/ppermute | solution.py:85
  199.7 7.9 %collective-permute-start.23 = (bf16[2,3,32,512]{3,2,1,0:T(8,128)(2,1)S(1)}, bf16[2,3,32,512]{3,2,1,0:T(8,128)(2,1)S(1)}, u32[]{:S(2)}, u32[]{:S(2)}) collective-permute-start(bf16[2,3,32,512]{3,2,1,0:T(8,128)(2,1)S(1)} %collective-permute-done.21), channel_id=1, source_target_pairs={{0,1},{1,2},{2,3},{3,4},{4,5},{5,6},{6,7},{7,8},{8,9},{9,10},{10,1... | collective-permute-start | bytes 589832 | tf_op jit(solution)/shard_map/ppermute | solution.py:78
  199.7 7.9 %collective-permute-start.24 = (bf16[2,3,32,512]{3,2,1,0:T(8,128)(2,1)S(1)}, bf16[2,3,32,512]{3,2,1,0:T(8,128)(2,1)S(1)}, u32[]{:S(2)}, u32[]{:S(2)}) collective-permute-start(bf16[2,3,32,512]{3,2,1,0:T(8,128)(2,1)S(1)} %collective-permute-done.22), channel_id=1, source_target_pairs={{0,15},{1,0},{2,1},{3,2},{4,3},{5,4},{6,5},{7,6},{8,7},{9,8},{10,9... | collective-permute-start | bytes 589832 | tf_op jit(solution)/shard_map/ppermute | solution.py:85
  207.6 7.9 %collective-permute-start.25 = (bf16[2,3,32,512]{3,2,1,0:T(8,128)(2,1)S(1)}, bf16[2,3,32,512]{3,2,1,0:T(8,128)(2,1)S(1)}, u32[]{:S(2)}, u32[]{:S(2)}) collective-permute-start(bf16[2,3,32,512]{3,2,1,0:T(8,128)(2,1)S(1)} %collective-permute-done.23), channel_id=1, source_target_pairs={{0,1},{1,2},{2,3},{3,4},{4,5},{5,6},{6,7},{7,8},{8,9},{9,10},{10,1... | collective-permute-start | bytes 589832 | tf_op jit(solution)/shard_map/ppermute | solution.py:78
  207.6 7.9 %collective-permute-start.26 = (bf16[2,3,32,512]{3,2,1,0:T(8,128)(2,1)S(1)}, bf16[2,3,32,512]{3,2,1,0:T(8,128)(2,1)S(1)}, u32[]{:S(2)}, u32[]{:S(2)}) collective-permute-start(bf16[2,3,32,512]{3,2,1,0:T(8,128)(2,1)S(1)} %collective-permute-done.24), channel_id=1, source_target_pairs={{0,15},{1,0},{2,1},{3,2},{4,3},{5,4},{6,5},{7,6},{8,7},{9,8},{10,9... | collective-permute-start | bytes 589832 | tf_op jit(solution)/shard_map/ppermute | solution.py:85
  215.5 7.8 %collective-permute-start.27 = (bf16[2,3,32,512]{3,2,1,0:T(8,128)(2,1)S(1)}, bf16[2,3,32,512]{3,2,1,0:T(8,128)(2,1)S(1)}, u32[]{:S(2)}, u32[]{:S(2)}) collective-permute-start(bf16[2,3,32,512]{3,2,1,0:T(8,128)(2,1)S(1)} %collective-permute-done.25), channel_id=1, source_target_pairs={{0,1},{1,2},{2,3},{3,4},{4,5},{5,6},{6,7},{7,8},{8,9},{9,10},{10,1... | collective-permute-start | bytes 589832 | tf_op jit(solution)/shard_map/ppermute | solution.py:78
  215.5 7.8 %collective-permute-start.28 = (bf16[2,3,32,512]{3,2,1,0:T(8,128)(2,1)S(1)}, bf16[2,3,32,512]{3,2,1,0:T(8,128)(2,1)S(1)}, u32[]{:S(2)}, u32[]{:S(2)}) collective-permute-start(bf16[2,3,32,512]{3,2,1,0:T(8,128)(2,1)S(1)} %collective-permute-done.26), channel_id=1, source_target_pairs={{0,15},{1,0},{2,1},{3,2},{4,3},{5,4},{6,5},{7,6},{8,7},{9,8},{10,9... | collective-permute-start | bytes 589832 | tf_op jit(solution)/shard_map/ppermute | solution.py:85
  220.0 12.5 %copy-start.3 = (bf16[256,1024]{1,0:T(8,128)(2,1)S(1)}, bf16[256,1024]{1,0:T(8,128)(2,1)}, u32[]{:S(2)}) copy-start(bf16[256,1024]{1,0:T(8,128)(2,1)} %get-tuple-element.10) | copy-start | bytes 1572868
  223.3 7.8 %collective-permute-start.29 = (bf16[2,3,32,512]{3,2,1,0:T(8,128)(2,1)S(1)}, bf16[2,3,32,512]{3,2,1,0:T(8,128)(2,1)S(1)}, u32[]{:S(2)}, u32[]{:S(2)}) collective-permute-start(bf16[2,3,32,512]{3,2,1,0:T(8,128)(2,1)S(1)} %collective-permute-done.27), channel_id=1, source_target_pairs={{0,1},{1,2},{2,3},{3,4},{4,5},{5,6},{6,7},{7,8},{8,9},{9,10},{10,1... | collective-permute-start | bytes 589832 | tf_op jit(solution)/shard_map/ppermute | solution.py:78
  231.5 1.7 copy-start.12
  232.5 1.1 copy-start.11
  233.2 0.8 copy-start.10
  233.6 0.9 copy-start.9
  234.0 0.9 copy-start.8
  234.5 0.9 copy-start.7
Sparse Core Ops, SparseCore 0:
  83.8 82.7 reduce-scatter.2
  239.9 82.3 reduce-scatter.4
